TPU v7x, 32 devices: a whole 2x2x4 slice. The times are simulated.
32 devices in a mesh: dp: 8 (over y, x, core), tensor: 4 (over z).
Axes of the slice: x: 2, y: 2, z: 4, core: 2. Of those that a mesh axis runs over, the one named last changes fastest.
Arguments:
- acts: bfloat16 [4096, 2048], P('dp', 'tensor'), may hold values from -6 to 6
- out_grads: bfloat16 [4096, 8192], P('dp', 'tensor'), may hold values from -6 to 6
- basis_out: bfloat16 [8192, 8192], P('tensor'), may hold values from -0.0625 to 0.0625
- basis_in: bfloat16 [2048, 2048], P('tensor'), may hold values from -0.125 to 0.125
- slot_sequence: int32 [16], replicated, may hold values from 0 to 15, each once
- seq_lengths: int32 [16], replicated, may hold values from 1 to 256, 2560 in all
Outputs:
- eigenvalues: float32 [8192, 2048], P('tensor', 'dp')
Inputs may be any that keep to these rules, and one draw needn't show every extreme that they name: `slot_sequence`: every sequence number appears exactly once. `seq_lengths`: the largest count is exactly 256.
All inputs are finite; a program needn't handle non-finite values.
Results may differ from a plain program's by a relative error of at most 0.0018.
Values may be sent and summed in bfloat16 or wider, within the bound.
No kernel may reach another device: no remote copies, remote signals or barrier semaphores. Data moves between devices by JAX's collectives and lax.ppermute only.
A program may use at most 128 MiB of HBM per device.

v0:
```python
import jax
import jax.numpy as jnp
from jax import lax
from jax.sharding import PartitionSpec as P

LEN = 256


def shards(acts, out_grads, basis_out, basis_in, slot_sequence, seq_lengths):
    tok_rows = acts.shape[0]
    local_seqs = tok_rows // LEN
    seq_total = seq_lengths.shape[0]
    group_index = lax.axis_index("dp")
    slot_ids = group_index * local_seqs + jnp.arange(local_seqs, dtype=jnp.int32)
    seq_numbers = jnp.arange(seq_total, dtype=jnp.int32)
    which_seq = jnp.sum(
        jnp.where(slot_ids[:, None] == seq_numbers[None, :], slot_sequence[None, :], 0), axis=1
    )
    slot_counts = jnp.sum(
        jnp.where(which_seq[:, None] == seq_numbers[None, :], seq_lengths[None, :], 0), axis=1
    )
    row_counts = jnp.repeat(slot_counts, LEN)
    positions = jnp.arange(tok_rows, dtype=jnp.int32) % LEN
    valid_mask = positions < row_counts
    masked = jnp.where(valid_mask[:, None], out_grads, jnp.zeros_like(out_grads))
    rot_sums = lax.psum_scatter(
        jnp.einsum("oi,to->it", basis_out, masked, preferred_element_type=jnp.float32),
        "tensor",
        scatter_dimension=0,
        tiled=True,
    )
    rot_grads = rot_sums.astype(jnp.bfloat16)
    whole_acts = lax.all_gather(acts, "tensor", axis=1, tiled=True)
    rot_acts = jnp.dot(
        whole_acts,
        lax.all_gather(basis_in, "tensor", axis=0, tiled=True),
        preferred_element_type=jnp.float32,
    ).astype(jnp.bfloat16)
    squares = jnp.zeros((rot_grads.shape[0], rot_acts.shape[1]), jnp.float32)
    for slot_pos in range(local_seqs):
        grad_slot = rot_grads[:, slot_pos * LEN : (slot_pos + 1) * LEN]
        act_slot = rot_acts[slot_pos * LEN : (slot_pos + 1) * LEN]
        rotated = jnp.dot(grad_slot, act_slot, preferred_element_type=jnp.float32)
        squares = squares + rotated * rotated
    summed = lax.psum_scatter(squares, "dp", scatter_dimension=1, tiled=True)
    return summed / (seq_total * LEN)


def solution(mesh):
    return jax.shard_map(
        shards,
        mesh=mesh,
        in_specs=(
            P("dp", "tensor"),
            P("dp", "tensor"),
            P("tensor", None),
            P("tensor", None),
            P(),
            P(),
        ),
        out_specs=P("tensor", "dp"),
        check_vma=False,
    )
```

profile of v0, /device:TPU:0, one launch (start us, length us, event | category | flops | bytes accessed | tf_op | source)
XLA Modules:
  0.0 628.3 jit_solution(10822918368611207636)
XLA Ops:
  6.5 0.0 copy-start.2
  6.5 0.0 copy-start.3
  6.5 0.0 copy-start.1
  6.5 0.0 all-gather.3.cloned.1.call-start
  6.5 0.7 all-gather.3.cloned.1.call-update
  7.3 0.0 all-gather.5.cloned.1.call-start
  7.3 0.7 all-gather.5.cloned.1.call-update
  8.0 0.0 reduce-scatter.3.cloned.1.call-start
  8.1 0.0 copy-done.2
  8.1 0.2 fusion.12
  8.3 0.0 copy-done.3
  8.3 0.2 fusion.13
  8.5 0.1 broadcast_bitcast_fusion
  8.5 0.0 copy-done.1
  8.5 26.9 %convolution_bitcast_fusion = f32[8192,512]{0,1:T(8,128)} fusion(bf16[2048,8192]{1,0:T(8,128)(2,1)} %param.8, bf16[512,2048]{1,0:T(8,128)(2,1)S(1)} %copy-done.1, pred[512]{0:T(512)(128)(4,1)S(1)} %fusion.8), kind=kOutput, calls=%fused_computation.1 | convolution fusion | flops 17180917760 | bytes 52429312 | tf_op jit(solution)/shard_map/oi,to->it/dot_general | solution.py:27
  35.4 0.0 reduce-scatter.3.cloned.1.call-update
  35.5 0.2 reduce-scatter.5.cloned.1.call-start
  35.7 21.6 %all-gather.3.cloned.1.call-done = bf16[512,2048]{1,0:T(8,128)(2,1)} async-done(((bf16[512,512]{1,0:T(8,128)(2,1)}), bf16[512,2048]{1,0:T(8,128)(2,1)}) %all-gather.3.cloned.1.call-update) | async-done | bytes 2097168 | tf_op jit(solution)/shard_map/all_gather | solution.py:33
  57.3 150.0 %all-gather.5.cloned.1.call-done = bf16[2048,2048]{1,0:T(8,128)(2,1)} async-done(((bf16[512,2048]{1,0:T(8,128)(2,1)}), bf16[2048,2048]{1,0:T(8,128)(2,1)}) %all-gather.5.cloned.1.call-update) | async-done | bytes 8388624 | tf_op jit(solution)/shard_map/all_gather | solution.py:36
  207.3 9.8 %convolution_convert_fusion = bf16[512,2048]{1,0:T(8,128)(2,1)} fusion(bf16[512,2048]{1,0:T(8,128)(2,1)} %all-gather.3.cloned.1.call-done, bf16[2048,2048]{1,0:T(8,128)(2,1)} %all-gather.5.cloned.1.call-done), kind=kOutput, calls=%fused_computation.2 | convolution fusion | flops 4296015872 | bytes 12582912 | tf_op jit(solution)/shard_map/dot_general | solution.py:34
  217.2 271.2 %reduce-scatter.3.cloned.1.call-done = f32[2048,512]{0,1:T(8,128)} async-done(((f32[8192,512]{0,1:T(8,128)}), f32[2048,512]{0,1:T(8,128)}) %reduce-scatter.3.cloned.1.call-update) | async-done | bytes 4194320 | tf_op jit(solution)/shard_map/reduce_scatter | solution.py:26
  488.4 0.0 copy-start
  488.4 2.6 convert_element_type.6
  491.0 0.2 copy-done
  491.2 2.4 fusion.4
  493.6 8.3 %multiply_add_fusion = f32[2048,2048]{1,0:T(8,128)} fusion(f32[2048,2048]{1,0:T(8,128)S(1)} %fusion.4, bf16[512,2048]{1,0:T(8,128)(2,1)} %convolution_convert_fusion, bf16[2048,512]{0,1:T(8,128)(2,1)S(1)} %convert_element_type.6), kind=kOutput, calls=%fused_computation | convolution fusion | flops 2160066560 | bytes 35651584 | tf_op jit(solution)/shard_map/dot_general | solution.py:43
  501.9 0.0 reduce-scatter.5.cloned.1.call-update
  501.9 116.8 %reduce-scatter.5.cloned.1.call-done = f32[2048,256]{1,0:T(8,128)} async-done(((f32[2048,2048]{1,0:T(8,128)}), f32[2048,256]{1,0:T(8,128)}) %reduce-scatter.5.cloned.1.call-update) | async-done | bytes 2097168 | tf_op jit(solution)/shard_map/reduce_scatter | solution.py:45
  618.7 3.0 broadcast_multiply_fusion
  (3 shorter events, 0.0 us)
Async XLA Ops:
  6.5 1.5 copy-start.2
  6.5 1.7 copy-start.3
  6.5 2.0 copy-start.1
  6.5 50.8 %all-gather.3.cloned.1.call-start = ((), (), s32[]{:S(2)}) async-start(), calls=%async_computation.3 | async-start | bytes 2621440 | tf_op jit(solution)/shard_map/all_gather | solution.py:33
  7.3 200.1 %all-gather.5.cloned.1.call-start = ((), (), s32[]{:S(2)}) async-start(), calls=%async_computation.4 | async-start | bytes 10485760 | tf_op jit(solution)/shard_map/all_gather | solution.py:36
  8.0 480.3 %reduce-scatter.3.cloned.1.call-start = ((), (), s32[]{:S(2)}) async-start(), calls=%async_computation.2 | async-start | bytes 20971520 | tf_op jit(solution)/shard_map/reduce_scatter | solution.py:26
  35.5 583.3 %reduce-scatter.5.cloned.1.call-start = ((), (), s32[]{:S(2)}) async-start(), calls=%async_computation.5 | async-start | bytes 18874368 | tf_op jit(solution)/shard_map/reduce_scatter | solution.py:45
  488.4 2.9 copy-start
Sparse Core Ops, SparseCore 0:
  8.9 48.3 all-gather.2
  58.9 148.4 all-gather.4
  209.7 278.6 reduce-scatter.2
  502.1 116.6 reduce-scatter.4
where the time goes:
time: 628 us
  waiting for transfers between devices  561 us (89%)
  matrix products  47.4 us (8%)
  between operations  13.2 us (2%)
    reduce_scatter x1, waiting for transfers between devices, shards(): lax.psum_scatter(jnp.einsum('oi,to->it', basis_out, masked, preferred_ele...  271 us
    all_gather x1, waiting for transfers between devices, shards(): lax.all_gather(basis_in, 'tensor', axis=0, tiled=True)  150 us
    reduce_scatter x1, waiting for transfers between devices, shards(): summed = lax.psum_scatter(squares, 'dp', scatter_dimension=1, tiled=True)  117 us
    dot_general x1, matrix products, shards(): jnp.einsum('oi,to->it', basis_out, masked, preferred_element_type=jnp.flo...  26.9 us
    all_gather x1, waiting for transfers between devices, shards(): whole_acts = lax.all_gather(acts, 'tensor', axis=1, tiled=True)  21.6 us
  transfers between devices with their start and end apart: 4, of which 4 were waited for; matrix products, arithmetic and copies ran while one was open for 6% of the time, Pallas kernels for 0%

commit v1 on v0

--- a/solution.py
+++ b/solution.py
@@ -4,6 +4,28 @@
 from jax.sharding import PartitionSpec as P
 
 LEN = 256
+
+
+def in_order(pieces, dim):
+    pieces = jnp.moveaxis(pieces, 0, dim)
+    lengths = pieces.shape
+    return pieces.reshape(*lengths[:dim], lengths[dim] * lengths[dim + 1], *lengths[dim + 2 :])
+
+
+def ring_gather(x, axis, dim):
+    peers = lax.axis_size(axis)
+    pairs = [(i, (i + 1) % peers) for i in range(peers)]
+    back = [(b, a) for a, b in pairs]
+    lower, upper = ([], [])
+    for step in range(peers - 1):
+        if step % 2 == 0:
+            lower.append(lax.ppermute(lower[-1] if lower else x, axis, pairs))
+        else:
+            upper.append(lax.ppermute(upper[-1] if upper else x, axis, back))
+    parts = jnp.stack([*lower[::-1], x, *upper])
+    shift = lax.axis_index(axis) - len(lower)
+    parts = parts[(jnp.arange(peers) - shift) % peers]
+    return in_order(parts, dim)
 
 
 def shards(acts, out_grads, basis_out, basis_in, slot_sequence, seq_lengths):
@@ -32,9 +54,7 @@
     rot_grads = rot_sums.astype(jnp.bfloat16)
     whole_acts = lax.all_gather(acts, "tensor", axis=1, tiled=True)
     rot_acts = jnp.dot(
-        whole_acts,
-        lax.all_gather(basis_in, "tensor", axis=0, tiled=True),
-        preferred_element_type=jnp.float32,
+        whole_acts, ring_gather(basis_in, "tensor", 0), preferred_element_type=jnp.float32
     ).astype(jnp.bfloat16)
     squares = jnp.zeros((rot_grads.shape[0], rot_acts.shape[1]), jnp.float32)
     for slot_pos in range(local_seqs):

time: 628 us -> 605 us (0.963)
  waiting for transfers between devices: 561 us -> 501 us
  local copies, waits for them, and re-layouts: 0.29 us -> 16.6 us
  other arithmetic: 6.06 us -> 19.5 us
    ppermute x0 -> x3, waiting for transfers between devices: none -> 223 us  [the longest x1 115 us: ring_gather(): upper.append(lax.ppermute(upper[-1] if upper else x, axis, back))]
    all_gather x1 -> x0, waiting for transfers between devices: 150 us -> none  [shards(): lax.all_gather(basis_in, 'tensor', axis=0, tiled=True)]
    reduce_scatter x1, waiting for transfers between devices: 271 us -> 160 us  [shards(): lax.psum_scatter(jnp.einsum('oi,to->it', basis_out, masked, preferred_ele...]
    all_gather x1, waiting for transfers between devices: 21.6 us -> 0.01 us  [shards(): whole_acts = lax.all_gather(acts, 'tensor', axis=1, tiled=True)]
    gather x0 -> x3, local copies, waits for them, and re-layouts: none -> 13.7 us  [ring_gather(): parts = parts[(jnp.arange(peers) - shift) % peers]]
    unnamed x0 -> x1, other arithmetic: none -> 8.24 us
  transfers between devices with their start and end apart: 4 -> 6, of which waited for: 4 -> 5; matrix products, arithmetic and copies ran while one was open for 6% -> 11% of each run, Pallas kernels for 0% -> 0%
where the time goes in v1:
time: 605 us
  waiting for transfers between devices  501 us (83%)
  matrix products  49.6 us (8%)
  other arithmetic  19.5 us (3%)
  local copies, waits for them, and re-layouts  16.6 us (3%)
  between operations  13.2 us (2%)
    reduce_scatter x1, waiting for transfers between devices, shards(): lax.psum_scatter(jnp.einsum('oi,to->it', basis_out, masked, preferred_ele...  160 us
    reduce_scatter x1, waiting for transfers between devices, shards(): summed = lax.psum_scatter(squares, 'dp', scatter_dimension=1, tiled=True)  117 us
    ppermute x1, waiting for transfers between devices, ring_gather(): upper.append(lax.ppermute(upper[-1] if upper else x, axis, back))  115 us
    ppermute x2, waiting for transfers between devices, ring_gather(): lower.append(lax.ppermute(lower[-1] if lower else x, axis, pairs))  108 us
    dot_general x1, matrix products, shards(): jnp.einsum('oi,to->it', basis_out, masked, preferred_element_type=jnp.flo...  27.5 us
    gather x3, local copies, waits for them, and re-layouts, ring_gather(): parts = parts[(jnp.arange(peers) - shift) % peers]  13.7 us
    dot_general x2, matrix products, shards(): rotated = jnp.dot(grad_slot, act_slot, preferred_element_type=jnp.float32)  12.2 us
  transfers between devices with their start and end apart: 6, of which 5 were waited for; matrix products, arithmetic and copies ran while one was open for 11% of the time, Pallas kernels for 0%

profile of v1, /device:TPU:0, one launch (start us, length us, event | category | flops | bytes accessed | tf_op | source)
XLA Modules:
  0.0 605.1 jit_solution(10250723935793368517)
XLA Ops:
  6.5 0.0 all-gather.2.cloned.1.call-start
  6.5 0.7 all-gather.2.cloned.1.call-update
  7.3 0.0 reduce-scatter.3.cloned.1.call-start
  7.3 0.8 fusion.13
  8.2 0.8 fusion.14
  9.0 0.1 broadcast_bitcast_fusion
  9.1 27.5 %convolution_bitcast_fusion = f32[8192,512]{0,1:T(8,128)} fusion(bf16[2048,8192]{1,0:T(8,128)(2,1)} %param.8, bf16[512,2048]{1,0:T(8,128)(2,1)} %param.7, pred[512]{0:T(512)(128)(4,1)S(1)} %fusion.9), kind=kOutput, calls=%fused_computation.3 | convolution fusion | flops 17180917760 | bytes 52429312 | tf_op jit(solution)/shard_map/oi,to->it/dot_general | solution.py:49
  36.6 0.0 copy-start.2
  36.6 0.0 reduce-scatter.3.cloned.1.call-update
  36.6 0.0 reduce-scatter.5.cloned.1.call-start
  36.6 1.5 copy-done.2
  38.2 3.0 collective-permute-start
  41.2 2.0 collective-permute-start.2
  43.2 59.7 %collective-permute-done = bf16[512,2048]{1,0:T(8,128)(2,1)} collective-permute-done((bf16[512,2048]{1,0:T(8,128)(2,1)S(1)}, bf16[512,2048]{1,0:T(8,128)(2,1)}, u32[]{:S(2)}, u32[]{:S(2)}) %collective-permute-start) | collective-permute-done | bytes 2097184 | tf_op jit(solution)/shard_map/ppermute | solution.py:22
  103.0 0.0 collective-permute-start.1
  103.0 115.4 %collective-permute-done.2 = bf16[512,2048]{1,0:T(8,128)(2,1)} collective-permute-done((bf16[512,2048]{1,0:T(8,128)(2,1)S(1)}, bf16[512,2048]{1,0:T(8,128)(2,1)}, u32[]{:S(2)}, u32[]{:S(2)}) %collective-permute-start.2) | collective-permute-done | bytes 2097184 | tf_op jit(solution)/shard_map/ppermute | solution.py:24
  218.4 47.8 %collective-permute-done.1 = bf16[512,2048]{1,0:T(8,128)(2,1)} collective-permute-done((bf16[512,2048]{1,0:T(8,128)(2,1)}, bf16[512,2048]{1,0:T(8,128)(2,1)}, u32[]{:S(2)}, u32[]{:S(2)}) %collective-permute-start.1) | collective-permute-done | bytes 2097184 | tf_op jit(solution)/shard_map/ppermute | solution.py:22
  266.3 3.8 pad_maximum_fusion
  270.1 3.7 fusion.18
  273.8 4.9 gather_fusion
  278.8 5.1 gather_fusion.1
  283.8 8.2 %pad_maximum_fusion.1 = bf16[4,512,2048]{2,1,0:T(8,128)(2,1)} fusion(bf16[4,512,1024]{2,1,0:T(8,128)(2,1)} %gather_fusion.1, bf16[4,512,1024]{2,1,0:T(8,128)(2,1)} %gather_fusion), kind=kLoop, calls=%fused_computation.5 | loop fusion | flops 16777216 | bytes 16777216
  292.1 0.0 all-gather.2.cloned.1.call-done
  292.1 9.9 %fusion = bf16[512,2048]{0,1:T(8,128)(2,1)} fusion(bf16[2048,2048]{1,0:T(8,128)(2,1)} %bitcast.17, bf16[512,2048]{1,0:T(8,128)(2,1)} %all-gather.2.cloned.1.call-done), kind=kOutput, calls=%fused_computation.7 | convolution fusion | flops 4296015872 | bytes 12582912 | tf_op jit(solution)/shard_map/dot_general | solution.py:56
  302.0 160.4 %reduce-scatter.3.cloned.1.call-done = f32[2048,512]{0,1:T(8,128)} async-done(((f32[8192,512]{0,1:T(8,128)}), f32[2048,512]{0,1:T(8,128)}) %reduce-scatter.3.cloned.1.call-update) | async-done | bytes 4194320 | tf_op jit(solution)/shard_map/reduce_scatter | solution.py:48
  462.3 0.0 copy-start.1
  462.3 2.6 convert_element_type.9
  465.0 0.0 copy-start
  465.0 1.3 copy-done
  466.3 0.0 copy-done.1
  466.3 2.4 fusion.5
  468.7 9.8 %multiply_add_fusion = f32[2048,2048]{1,0:T(8,128)} fusion(f32[2048,2048]{1,0:T(8,128)S(1)} %fusion.5, bf16[512,2048]{0,1:T(8,128)(2,1)} %fusion, bf16[2048,512]{0,1:T(8,128)(2,1)} %copy-done), kind=kOutput, calls=%fused_computation.2 | convolution fusion | flops 2160066560 | bytes 35651584 | tf_op jit(solution)/shard_map/dot_general | solution.py:63
  478.5 0.0 reduce-scatter.5.cloned.1.call-update
  478.6 117.0 %reduce-scatter.5.cloned.1.call-done = f32[2048,256]{1,0:T(8,128)} async-done(((f32[2048,2048]{1,0:T(8,128)}), f32[2048,256]{1,0:T(8,128)}) %reduce-scatter.5.cloned.1.call-update) | async-done | bytes 2097168 | tf_op jit(solution)/shard_map/reduce_scatter | solution.py:65
  595.6 3.0 broadcast_multiply_fusion
  (5 shorter events, 0.0 us)
Async XLA Ops:
  6.5 285.5 %all-gather.2.cloned.1.call-start = ((), (), s32[]{:S(2)}) async-start(), calls=%async_computation.3 | async-start | bytes 2621440 | tf_op jit(solution)/shard_map/all_gather | solution.py:55
  7.3 455.1 %reduce-scatter.3.cloned.1.call-start = ((), (), s32[]{:S(2)}) async-start(), calls=%async_computation.2 | async-start | bytes 20971520 | tf_op jit(solution)/shard_map/reduce_scatter | solution.py:48
  36.6 1.6 copy-start.2
  36.6 559.0 %reduce-scatter.5.cloned.1.call-start = ((), (), s32[]{:S(2)}) async-start(), calls=%async_computation.4 | async-start | bytes 18874368 | tf_op jit(solution)/shard_map/reduce_scatter | solution.py:65
  38.2 64.8 %collective-permute-start = (bf16[512,2048]{1,0:T(8,128)(2,1)S(1)}, bf16[512,2048]{1,0:T(8,128)(2,1)}, u32[]{:S(2)}, u32[]{:S(2)}) collective-permute-start(bf16[512,2048]{1,0:T(8,128)(2,1)S(1)} %copy-done.2), channel_id=1, source_target_pairs={{0,1},{1,2},{2,3},{3,0},{4,5},{5,6},{6,7},{7,4},{8,9},{9,10},{10,1... | collective-permute-start | bytes 6291464 | tf_op jit(solution)/shard_map/ppermute | solution.py:22
  41.2 177.2 %collective-permute-start.2 = (bf16[512,2048]{1,0:T(8,128)(2,1)S(1)}, bf16[512,2048]{1,0:T(8,128)(2,1)}, u32[]{:S(2)}, u32[]{:S(2)}) collective-permute-start(bf16[512,2048]{1,0:T(8,128)(2,1)S(1)} %copy-done.2), channel_id=1, source_target_pairs={{1,0},{2,1},{3,2},{0,3},{5,4},{6,5},{7,6},{4,7},{9,8},{10,9},{11,1... | collective-permute-start | bytes 6291464 | tf_op jit(solution)/shard_map/ppermute | solution.py:24
  103.0 163.3 %collective-permute-start.1 = (bf16[512,2048]{1,0:T(8,128)(2,1)}, bf16[512,2048]{1,0:T(8,128)(2,1)}, u32[]{:S(2)}, u32[]{:S(2)}) collective-permute-start(bf16[512,2048]{1,0:T(8,128)(2,1)} %collective-permute-done), channel_id=1, source_target_pairs={{0,1},{1,2},{2,3},{3,0},{4,5},{5,6},{6,7},{7,4},{8,9},{9,10},{10,1... | collective-permute-start | bytes 6291464 | tf_op jit(solution)/shard_map/ppermute | solution.py:22
  462.3 4.0 copy-start.1
  465.0 1.3 copy-start
Sparse Core Ops, SparseCore 0:
  8.9 99.7 all-gather.1
  111.1 351.1 reduce-scatter.2
  478.7 116.8 reduce-scatter.4
